TPU v7x, 32 devices: a whole 2x2x4 slice. The times are simulated.
32 devices in a mesh: row: 16 (over z, y, x), col: 2 (over core).
Axes of the slice: x: 2, y: 2, z: 4, core: 2. Of those that a mesh axis runs over, the one named last changes fastest.
Arguments:
- matrix: bfloat16 [16384, 2048], P('row', 'col'), may hold values from -6 to 6
- fill_mask: int32 [64, 16], P('row', 'col'), may hold values from 0 to 1, as said below
- col_rows: int32 [16], replicated, may hold values from 0 to 127, as said below
- inverses: bfloat16 [2, 128, 128], replicated, may hold values from -0.05 to 0.15625
Outputs:
- factor: bfloat16 [16384, 2048], P('row', 'col')
Inputs may be any that keep to these rules, and one draw needn't show every extreme that they name: `fill_mask`: each column panel's density of filled blocks is drawn for that column from 1/8 to 8/8. `col_rows`: exactly 1 entries lie in each aligned run of 8 slabs.
All inputs are finite; a program needn't handle non-finite values.
Results may differ from a plain program's by a relative error of at most 0.0035.
Values may be sent and summed in bfloat16 or wider, within the bound.
No kernel may reach another device: no remote copies, remote signals or barrier semaphores. Data moves between devices by JAX's collectives and lax.ppermute only.
A program may use at most 64 MiB of HBM per device.

v0:
```python
import jax
import jax.numpy as jnp
from jax import lax
from jax.sharding import PartitionSpec as P

RB = 256
PW = 128


def from_root(shard, axis, root):
    mine = lax.axis_index(axis) == root
    return lax.psum(jnp.where(mine, shard, jnp.zeros_like(shard)), axis)


def contract(left, right):
    return lax.dot_general(
        left, right, (((1,), (1,)), ((), ())), preferred_element_type=jnp.float32
    )


def fetch_slabs(panel_tiles, col_rows):
    row_count = lax.axis_size("row")
    row_index = lax.axis_index("row")
    col_index = lax.axis_index("col")
    slab_tiles = panel_tiles.reshape(-1, PW, PW)
    per_device = slab_tiles.shape[0]
    all_cols = col_rows.shape[0]
    col_panels = all_cols // lax.axis_size("col")
    owner_row = col_rows // per_device
    slab_place = col_rows % per_device
    per_owner = all_cols // row_count
    position = jnp.arange(all_cols, dtype=jnp.int32)
    earlier = (owner_row[None, :] == owner_row[:, None]) & (position[None, :] < position[:, None])
    slab_rank = jnp.sum(earlier.astype(jnp.int32), axis=1)
    is_owned = (owner_row == row_index).astype(jnp.int32)
    rank_match = (slab_rank[:, None] == jnp.arange(per_owner, dtype=jnp.int32)[None, :]).astype(
        jnp.int32
    ) * is_owned[:, None]
    place_match = (slab_place[:, None] == jnp.arange(per_device, dtype=jnp.int32)[None, :]).astype(
        jnp.int32
    )
    select_table = jnp.dot(rank_match.T, place_match).astype(jnp.bfloat16)
    owned_slabs = jnp.einsum(
        "qs,sij->qij", select_table, slab_tiles, preferred_element_type=jnp.float32
    ).astype(jnp.bfloat16)
    everyone = lax.all_gather(owned_slabs, "row", axis=0, tiled=True)
    wanted_owner = lax.dynamic_slice_in_dim(owner_row, col_index * col_panels, col_panels)
    wanted_rank = lax.dynamic_slice_in_dim(slab_rank, col_index * col_panels, col_panels)
    gather_slot = wanted_owner * per_owner + wanted_rank
    pick_table = (
        gather_slot[:, None] == jnp.arange(row_count * per_owner, dtype=jnp.int32)[None, :]
    ).astype(jnp.bfloat16)
    result = jnp.einsum(
        "tq,qij->tij", pick_table, everyone, preferred_element_type=jnp.float32
    ).astype(jnp.bfloat16)
    return result


def shards(matrix, fill_mask, col_rows, inverses):
    col_index = lax.axis_index("col")
    local_rows = matrix.shape[0]
    width = matrix.shape[1]
    col_panels = fill_mask.shape[1]
    rows_mask = jnp.repeat(fill_mask.astype(jnp.float32), RB, axis=0)
    first_local = (
        jnp.dot(matrix[:, :PW], jnp.triu(inverses[0]), preferred_element_type=jnp.float32)
        * rows_mask[:, 0:1]
    ).astype(jnp.bfloat16)
    first_panel = from_root(first_local, "col", 0)
    diag_first = fetch_slabs(first_panel, col_rows)
    column_sum = matrix[:, :PW].astype(jnp.float32) - contract(first_panel, diag_first[0])
    panel_update = column_sum.astype(jnp.bfloat16)
    second_local = (
        jnp.dot(panel_update, jnp.triu(inverses[1]), preferred_element_type=jnp.float32)
        * rows_mask[:, 0:1]
    ).astype(jnp.bfloat16)
    second_panel = from_root(second_local, "col", 1)
    diag_second = fetch_slabs(second_panel, col_rows)
    both_panels = jnp.concatenate((first_panel, second_panel), axis=1)
    both_diag = jnp.concatenate((diag_first, diag_second), axis=2).reshape(-1, 2 * PW)
    schur_sum = matrix.astype(jnp.float32) - contract(both_panels, both_diag)
    masked = (
        (schur_sum.reshape(local_rows, col_panels, PW) * rows_mask[:, :, None])
        .astype(jnp.bfloat16)
        .reshape(local_rows, width)
    )
    leading = jnp.where(
        col_index == 0, first_panel, jnp.where(col_index == 1, second_panel, masked[:, :PW])
    )
    return jnp.concatenate((leading, masked[:, PW:]), axis=1)


def solution(mesh):
    in_specs = (P("row", "col"), P("row", "col"), P(), P())
    out_specs = P("row", "col")
    return jax.shard_map(shards, mesh=mesh, in_specs=in_specs, out_specs=out_specs, check_vma=False)
```

profile of v0, /device:TPU:0, one launch (start us, length us, event | category | flops | bytes accessed | tf_op | source)
XLA Modules:
  0.0 149.6 jit_solution(10960983689356108654)
XLA Ops:
  6.5 0.0 copy-start.2
  6.5 0.0 all-reduce.3.cloned.1.call-start
  6.5 0.7 convert_element_type.58
  7.3 0.1 broadcast_in_dim.8
  7.3 2.0 %fusion.6 = bf16[1024,128]{0,1:T(8,128)(2,1)} fusion(f32[1024]{0:T(1024)S(1)} %bitcast.68, pred[]{:T(512)S(6)} %eq.32, bf16[1024,1024]{1,0:T(8,128)(2,1)} %param.4, bf16[2,128,128]{2,1,0:T(8,128)(2,1)} %param.7, s32[128]{0:T(128)S(1)} %iota_add_fusion), kind=kOutput, calls=%fused_computation.13 | convolution fusion | flops 33980416 | bytes 561665 | tf_op jit(solution)/shard_map/dot_general | solution.py:66
  9.3 0.0 all-reduce.3.cloned.1.call-update
  9.4 0.0 all-reduce.5.cloned.1.call-start
  9.4 0.7 and_select_fusion.1
  10.1 0.2 convert_reduce_fusion
  10.3 0.1 dynamic-slice_add_fusion
  10.3 0.2 convolution_bitcast_fusion
  10.5 20.1 %all-reduce.3.cloned.1.call-done = bf16[1024,128]{0,1:T(8,128)(2,1)} async-done(((bf16[1024,128]{0,1:T(8,128)(2,1)}), bf16[1024,128]{0,1:T(8,128)(2,1)}) %all-reduce.3.cloned.1.call-update) | async-done | bytes 262160 | tf_op jit(solution)/shard_map/psum | solution.py:12
  30.7 0.0 copy-start
  30.7 1.1 copy.24
  31.8 0.2 fusion.47
  32.0 0.1 copy.20
  32.1 44.0 %all-gather = bf16[2048,128]{1,0:T(8,128)(2,1)S(1)} all-gather(bf16[128,128]{1,0:T(8,128)(2,1)S(1)} %bitcast.66), channel_id=2, replica_groups=mesh['row'=16,'col'=2] {'row'}, dimensions={0}, use_global_device_ids=true | all-gather | bytes 557056 | tf_op jit(solution)/shard_map/all_gather | solution.py:46
  76.1 0.4 convolution_convert_fusion.1
  76.5 0.0 copy-done.2
  76.5 0.0 copy-done
  76.6 2.1 %fusion.4 = bf16[1024,128]{0,1:T(8,128)(2,1)} fusion(bf16[1024,128]{0,1:T(8,128)(2,1)S(1)} %copy-done, f32[1024]{0:T(1024)S(1)} %bitcast.69, pred[]{:T(512)S(6)} %eq.33, bf16[1024,1024]{1,0:T(8,128)(2,1)} %param.4, bf16[1,128,128]{2,0,1:T(2,128)(2,1)S(1)} %slice.31, bf16[2,128,128]{2,1,0:T(8,128)(2,1)S(1)} %copy-done.2, s32[128]{0:T(128)S(1)} %iota_add_fusion), kind=kOutput, calls=%fused_computation.11 | convolution fusion | flops 67928064 | bytes 889345 | tf_op jit(solution)/shard_map/dot_general | solution.py:74
  78.7 0.0 all-reduce.5.cloned.1.call-update
  78.7 2.9 %copy.16 = bf16[1024,1024]{0,1:T(8,128)(2,1)S(1)} copy(bf16[1024,1024]{1,0:T(8,128)(2,1)} %param.4) | data formatting | bytes 4194304 | tf_op args[0]
  81.6 11.4 %all-reduce.5.cloned.1.call-done = bf16[1024,128]{0,1:T(8,128)(2,1)} async-done(((bf16[1024,128]{0,1:T(8,128)(2,1)}), bf16[1024,128]{0,1:T(8,128)(2,1)}) %all-reduce.5.cloned.1.call-update) | async-done | bytes 262160 | tf_op jit(solution)/shard_map/psum | solution.py:12
  93.0 0.0 copy-start.1
  93.0 1.1 copy.25
  94.1 0.2 fusion.48
  94.3 0.1 copy.22
  94.4 44.0 %all-gather.1 = bf16[2048,128]{1,0:T(8,128)(2,1)S(1)} all-gather(bf16[128,128]{1,0:T(8,128)(2,1)S(1)} %bitcast.67), channel_id=3, replica_groups=mesh['row'=16,'col'=2] {'row'}, dimensions={0}, use_global_device_ids=true | all-gather | bytes 557056 | tf_op jit(solution)/shard_map/all_gather | solution.py:46
  138.4 0.4 convolution_convert_fusion
  138.8 0.1 pad_maximum_fusion.1
  138.9 0.1 copy.18
  139.0 0.0 copy-done.1
  139.0 0.7 fusion
  139.8 0.1 slice.33
  139.9 0.1 fusion.13
  140.0 0.2 pad_maximum_fusion
  140.2 2.6 %copy.19 = bf16[1024,1024]{1,0:T(8,128)(2,1)} copy(bf16[1024,1024]{0,1:T(8,128)(2,1)S(1)} %pad_maximum_fusion) | data formatting | bytes 4194304 | tf_op jit(solution)/shard_map/concatenate | solution.py:90
  (3 shorter events, 0.0 us)
Async XLA Ops:
  6.5 70.0 %copy-start.2 = (bf16[2,128,128]{2,1,0:T(8,128)(2,1)S(1)}, bf16[2,128,128]{2,1,0:T(8,128)(2,1)}, u32[]{:S(2)}) copy-start(bf16[2,128,128]{2,1,0:T(8,128)(2,1)} %param.7) | copy-start | bytes 196612
  6.5 24.1 %all-reduce.3.cloned.1.call-start = ((), (), s32[]{:S(2)}) async-start(), calls=%async_computation | async-start | bytes 524288 | tf_op jit(solution)/shard_map/psum | solution.py:12
  9.4 83.7 %all-reduce.5.cloned.1.call-start = ((), (), s32[]{:S(2)}) async-start(), calls=%async_computation.1 | async-start | bytes 524288 | tf_op jit(solution)/shard_map/psum | solution.py:12
  30.7 45.9 %copy-start = (bf16[1024,128]{0,1:T(8,128)(2,1)S(1)}, bf16[1024,128]{0,1:T(8,128)(2,1)}, u32[]{:S(2)}) copy-start(bf16[1024,128]{0,1:T(8,128)(2,1)} %all-reduce.3.cloned.1.call-done) | copy-start | bytes 786436
  93.0 46.0 %copy-start.1 = (bf16[1024,128]{0,1:T(8,128)(2,1)S(1)}, bf16[1024,128]{0,1:T(8,128)(2,1)}, u32[]{:S(2)}) copy-start(bf16[1024,128]{0,1:T(8,128)(2,1)} %all-reduce.5.cloned.1.call-done) | copy-start | bytes 786436
Sparse Core Ops, SparseCore 0:
  9.7 20.9 all-reduce.2
  78.8 14.1 all-reduce.4
where the time goes:
time: 150 us
  blocking collectives  88 us (59%)
  waiting for transfers between devices  31.6 us (21%)
  between operations  13.5 us (9%)
  local copies, waits for them, and re-layouts  8.17 us (5%)
  matrix products  6.28 us (4%)
  other arithmetic  1.96 us (1%)
    all_gather x2, blocking collectives, fetch_slabs(): everyone = lax.all_gather(owned_slabs, 'row', axis=0, tiled=True)  88 us
    psum x2, waiting for transfers between devices, from_root(): return lax.psum(jnp.where(mine, shard, jnp.zeros_like(shard)), axis)  31.6 us
    unnamed x9, local copies, waits for them, and re-layouts  5.01 us
  transfers between devices with their start and end apart: 2, of which 2 were waited for; matrix products, arithmetic and copies ran while one was open for 3% of the time, Pallas kernels for 0%

commit v1 on v0

--- a/solution.py
+++ b/solution.py
@@ -5,6 +5,22 @@
 
 RB = 256
 PW = 128
+
+
+def product_in_turn(array, axis, dim, term):
+    size, here, width = (lax.axis_size(axis), lax.axis_index(axis), array.shape[dim])
+    right = [(i, (i + 1) % size) for i in range(size)]
+    left = [(i, (i - 1) % size) for i in range(size)]
+    middle = size // 2
+    from_left = from_right = array
+    total = term(array, here * width)
+    for turn in range(1, middle + 1):
+        from_left = lax.ppermute(from_left, axis, right)
+        if turn < size - middle:
+            from_right = lax.ppermute(from_right, axis, left)
+            total = total + term(from_right, (here + turn) % size * width)
+        total = total + term(from_left, (here - turn) % size * width)
+    return total
 
 
 def from_root(shard, axis, root):
@@ -43,15 +59,22 @@
     owned_slabs = jnp.einsum(
         "qs,sij->qij", select_table, slab_tiles, preferred_element_type=jnp.float32
     ).astype(jnp.bfloat16)
-    everyone = lax.all_gather(owned_slabs, "row", axis=0, tiled=True)
     wanted_owner = lax.dynamic_slice_in_dim(owner_row, col_index * col_panels, col_panels)
     wanted_rank = lax.dynamic_slice_in_dim(slab_rank, col_index * col_panels, col_panels)
     gather_slot = wanted_owner * per_owner + wanted_rank
     pick_table = (
         gather_slot[:, None] == jnp.arange(row_count * per_owner, dtype=jnp.int32)[None, :]
     ).astype(jnp.bfloat16)
-    result = jnp.einsum(
-        "tq,qij->tij", pick_table, everyone, preferred_element_type=jnp.float32
+    result = product_in_turn(
+        owned_slabs,
+        "row",
+        0,
+        lambda shard_2, start: jnp.einsum(
+            "tq,qij->tij",
+            lax.dynamic_slice_in_dim(pick_table, start, shard_2.shape[0], axis=1),
+            shard_2,
+            preferred_element_type=jnp.float32,
+        ),
     ).astype(jnp.bfloat16)
     return result
 

time: 150 us -> 197 us (1.31)
  blocking collectives: 88 us -> 0 us
  starting transfers between devices: 0.04 us -> 80.9 us
  waiting for transfers between devices: 31.6 us -> 84.5 us
    all_gather x2 -> x0, blocking collectives: 88 us -> none  [fetch_slabs(): everyone = lax.all_gather(owned_slabs, 'row', axis=0, tiled=True)]
    ppermute x0 -> x30, starting transfers between devices: none -> 80.8 us  [the longest x14 80.6 us: product_in_turn(): from_right = lax.ppermute(from_right, axis, left)]
    ppermute x0 -> x30, waiting for transfers between devices: none -> 50.3 us  [the longest x16 41.1 us: product_in_turn(): from_left = lax.ppermute(from_left, axis, right)]
    psum x2, waiting for transfers between devices: 31.6 us -> 34.2 us  [from_root(): return lax.psum(jnp.where(mine, shard, jnp.zeros_like(shard)), axis)]
  transfers between devices with their start and end apart: 2 -> 32, of which waited for: 2 -> 23; matrix products, arithmetic and copies ran while one was open for 3% -> 2% of each run, Pallas kernels for 0% -> 0%
where the time goes in v1:
time: 197 us; the launch traced here: 196 us
  waiting for transfers between devices  84.5 us (43%)
  starting transfers between devices  80.9 us (41%)
  between operations  14 us (7%)
  local copies, waits for them, and re-layouts  7.94 us (4%)
  matrix products  5.49 us (3%)
  other arithmetic  3.53 us (2%)
    ppermute x14, starting transfers between devices, product_in_turn(): from_right = lax.ppermute(from_right, axis, left)  80.6 us
    ppermute x16, waiting for transfers between devices, product_in_turn(): from_left = lax.ppermute(from_left, axis, right)  41.1 us
    psum x2, waiting for transfers between devices, from_root(): return lax.psum(jnp.where(mine, shard, jnp.zeros_like(shard)), axis)  34.2 us
    ppermute x14, waiting for transfers between devices, product_in_turn(): from_right = lax.ppermute(from_right, axis, left)  9.13 us
    unnamed x9, local copies, waits for them, and re-layouts  4.92 us
  transfers between devices with their start and end apart: 32, of which 23 were waited for; matrix products, arithmetic and copies ran while one was open for 2% of the time, Pallas kernels for 0%

profile of v1, /device:TPU:0, one launch (start us, length us, event | category | flops | bytes accessed | tf_op | source)
XLA Modules:
  0.0 196.3 jit_solution(10537926311260747002)
XLA Ops:
  6.5 0.7 convert_element_type.58
  7.2 0.1 broadcast_in_dim.8
  7.3 2.0 %fusion.6 = bf16[1024,128]{0,1:T(8,128)(2,1)} fusion(f32[1024]{0:T(1024)S(1)} %bitcast.190, pred[]{:T(512)S(6)} %eq.115, bf16[1024,1024]{1,0:T(8,128)(2,1)} %param.4, bf16[2,128,128]{2,1,0:T(8,128)(2,1)} %param.7, s32[128]{0:T(128)S(1)} %iota_add_fusion), kind=kOutput, calls=%fused_computation.11 | convolution fusion | flops 33980416 | bytes 561665 | tf_op jit(solution)/shard_map/dot_general | solution.py:89
  9.3 0.0 all-reduce.5.cloned.1.call-start
  9.4 0.7 and_select_fusion.1
  10.1 0.2 convert_reduce_fusion
  10.2 0.2 convolution_bitcast_fusion
  10.4 0.1 dynamic-slice_add_fusion
  10.8 19.9 %all-reduce.3.cloned.1.call-done = bf16[1024,128]{0,1:T(8,128)(2,1)} async-done(((bf16[1024,128]{0,1:T(8,128)(2,1)}), bf16[1024,128]{0,1:T(8,128)(2,1)}) %all-reduce.3.cloned.1.call-update) | async-done | bytes 262160 | tf_op jit(solution)/shard_map/psum | solution.py:28
  30.7 1.1 copy.14
  31.8 0.2 fusion.72
  32.0 0.1 copy.11
  32.1 5.5 %collective-permute-start = (bf16[1,128,128]{2,1,0:T(8,128)(2,1)S(1)}, bf16[1,128,128]{2,1,0:T(8,128)(2,1)S(1)}, u32[]{:S(2)}, u32[]{:S(2)}) collective-permute-start(bf16[1,128,128]{2,1,0:T(8,128)(2,1)S(1)} %get-tuple-element.8), channel_id=1, source_target_pairs={{0,30},{2,0},{4,2},{6,4},{8,6},{10,8},{12,10},{14,12},{16,14},{18,... | collective-permute-start | bytes 98312 | tf_op jit(solution)/shard_map/ppermute | solution.py:20
  37.6 0.1 collective-permute-start.1
  37.7 1.5 collective-permute-done
  39.2 5.9 %collective-permute-start.2 = (bf16[1,128,128]{2,1,0:T(8,128)(2,1)S(1)}, bf16[1,128,128]{2,1,0:T(8,128)(2,1)S(1)}, u32[]{:S(2)}, u32[]{:S(2)}) collective-permute-start(bf16[1,128,128]{2,1,0:T(8,128)(2,1)S(1)} %collective-permute-done), channel_id=1, source_target_pairs={{0,30},{2,0},{4,2},{6,4},{8,6},{10,8},{12,10},{14,12},{16,14},{18,... | collective-permute-start | bytes 98312 | tf_op jit(solution)/shard_map/ppermute | solution.py:20
  45.1 0.1 collective-permute-done.1
  45.2 1.5 collective-permute-done.2
  46.7 5.9 %collective-permute-start.4 = (bf16[1,128,128]{2,1,0:T(8,128)(2,1)S(1)}, bf16[1,128,128]{2,1,0:T(8,128)(2,1)S(1)}, u32[]{:S(2)}, u32[]{:S(2)}) collective-permute-start(bf16[1,128,128]{2,1,0:T(8,128)(2,1)S(1)} %collective-permute-done.2), channel_id=1, source_target_pairs={{0,30},{2,0},{4,2},{6,4},{8,6},{10,8},{12,10},{14,12},{16,14},{18,... | collective-permute-start | bytes 98312 | tf_op jit(solution)/shard_map/ppermute | solution.py:20
  52.6 0.1 collective-permute-done.3
  52.7 1.5 collective-permute-done.4
  54.2 5.9 %collective-permute-start.6 = (bf16[1,128,128]{2,1,0:T(8,128)(2,1)S(1)}, bf16[1,128,128]{2,1,0:T(8,128)(2,1)S(1)}, u32[]{:S(2)}, u32[]{:S(2)}) collective-permute-start(bf16[1,128,128]{2,1,0:T(8,128)(2,1)S(1)} %collective-permute-done.4), channel_id=1, source_target_pairs={{0,30},{2,0},{4,2},{6,4},{8,6},{10,8},{12,10},{14,12},{16,14},{18,... | collective-permute-start | bytes 98312 | tf_op jit(solution)/shard_map/ppermute | solution.py:20
  60.1 0.1 collective-permute-done.5
  60.2 1.5 collective-permute-done.6
  61.7 5.9 %collective-permute-start.8 = (bf16[1,128,128]{2,1,0:T(8,128)(2,1)S(1)}, bf16[1,128,128]{2,1,0:T(8,128)(2,1)S(1)}, u32[]{:S(2)}, u32[]{:S(2)}) collective-permute-start(bf16[1,128,128]{2,1,0:T(8,128)(2,1)S(1)} %collective-permute-done.6), channel_id=1, source_target_pairs={{0,30},{2,0},{4,2},{6,4},{8,6},{10,8},{12,10},{14,12},{16,14},{18,... | collective-permute-start | bytes 98312 | tf_op jit(solution)/shard_map/ppermute | solution.py:20
  67.6 0.1 collective-permute-done.7
  67.7 1.5 collective-permute-done.8
  69.2 5.9 %collective-permute-start.10 = (bf16[1,128,128]{2,1,0:T(8,128)(2,1)S(1)}, bf16[1,128,128]{2,1,0:T(8,128)(2,1)S(1)}, u32[]{:S(2)}, u32[]{:S(2)}) collective-permute-start(bf16[1,128,128]{2,1,0:T(8,128)(2,1)S(1)} %collective-permute-done.8), channel_id=1, source_target_pairs={{0,30},{2,0},{4,2},{6,4},{8,6},{10,8},{12,10},{14,12},{16,14},{18,... | collective-permute-start | bytes 98312 | tf_op jit(solution)/shard_map/ppermute | solution.py:20
  75.1 0.1 collective-permute-done.9
  75.2 1.6 collective-permute-done.10
  76.9 6.1 %collective-permute-start.12 = (bf16[1,128,128]{2,1,0:T(8,128)(2,1)S(1)}, bf16[1,128,128]{2,1,0:T(8,128)(2,1)S(1)}, u32[]{:S(2)}, u32[]{:S(2)}) collective-permute-start(bf16[1,128,128]{2,1,0:T(8,128)(2,1)S(1)} %collective-permute-done.10), channel_id=1, source_target_pairs={{0,30},{2,0},{4,2},{6,4},{8,6},{10,8},{12,10},{14,12},{16,14},{18,... | collective-permute-start | bytes 98312 | tf_op jit(solution)/shard_map/ppermute | solution.py:20
  82.9 0.1 collective-permute-start.13
  83.0 7.5 %collective-permute-done.13 = bf16[1,128,128]{2,1,0:T(8,128)(2,1)S(1)} collective-permute-done((bf16[1,128,128]{2,1,0:T(8,128)(2,1)S(1)}, bf16[1,128,128]{2,1,0:T(8,128)(2,1)S(1)}, u32[]{:S(2)}, u32[]{:S(2)}) %collective-permute-start.13) | collective-permute-done | bytes 32800 | tf_op jit(solution)/shard_map/ppermute | solution.py:18
  90.5 7.5 %collective-permute-done.14 = bf16[1,128,128]{2,1,0:T(8,128)(2,1)S(1)} collective-permute-done((bf16[1,128,128]{2,1,0:T(8,128)(2,1)S(1)}, bf16[1,128,128]{2,1,0:T(8,128)(2,1)S(1)}, u32[]{:S(2)}, u32[]{:S(2)}) %collective-permute-start.14) | collective-permute-done | bytes 32800 | tf_op jit(solution)/shard_map/ppermute | solution.py:18
  98.0 0.7 add_convert_fusion.1
  98.7 2.1 %fusion.4 = bf16[1024,128]{0,1:T(8,128)(2,1)} fusion(bf16[1024,128]{0,1:T(8,128)(2,1)S(1)} %copy-done, f32[1024]{0:T(1024)S(1)} %bitcast.191, pred[]{:T(512)S(6)} %eq.116, bf16[1024,1024]{1,0:T(8,128)(2,1)} %param.4, bf16[8,128,128]{2,1,0:T(8,128)(2,1)S(1)} %add_convert_fusion.1, bf16[2,128,128]{2,1,0:T(8,128)(2,1)S(1)} %copy-done.2, s32[128]{0:T(128)S(1)} %iota_add_fusion), kind=kOutput, calls=%fused_computation.9 | convolution fusion | flops 67928064 | bytes 856577 | tf_op jit(solution)/shard_map/dot_general | solution.py:97
  100.9 14.3 %all-reduce.5.cloned.1.call-done = bf16[1024,128]{0,1:T(8,128)(2,1)} async-done(((bf16[1024,128]{0,1:T(8,128)(2,1)}), bf16[1024,128]{0,1:T(8,128)(2,1)}) %all-reduce.5.cloned.1.call-update) | async-done | bytes 262160 | tf_op jit(solution)/shard_map/psum | solution.py:28
  115.2 1.0 copy.15
  116.2 0.2 fusion.73
  116.4 0.1 copy.13
  116.5 5.5 %collective-permute-start.15 = (bf16[1,128,128]{2,1,0:T(8,128)(2,1)S(1)}, bf16[1,128,128]{2,1,0:T(8,128)(2,1)S(1)}, u32[]{:S(2)}, u32[]{:S(2)}) collective-permute-start(bf16[1,128,128]{2,1,0:T(8,128)(2,1)S(1)} %get-tuple-element.6), channel_id=1, source_target_pairs={{0,30},{2,0},{4,2},{6,4},{8,6},{10,8},{12,10},{14,12},{16,14},{18,... | collective-permute-start | bytes 98312 | tf_op jit(solution)/shard_map/ppermute | solution.py:20
  122.0 2.9 %copy.9 = bf16[1024,1024]{0,1:T(8,128)(2,1)S(1)} copy(bf16[1024,1024]{1,0:T(8,128)(2,1)} %param.4) | data formatting | bytes 4194304 | tf_op args[0]
  124.8 0.1 collective-permute-start.16
  124.9 5.6 %collective-permute-start.17 = (bf16[1,128,128]{2,1,0:T(8,128)(2,1)S(1)}, bf16[1,128,128]{2,1,0:T(8,128)(2,1)S(1)}, u32[]{:S(2)}, u32[]{:S(2)}) collective-permute-start(bf16[1,128,128]{2,1,0:T(8,128)(2,1)S(1)} %collective-permute-done.15), channel_id=1, source_target_pairs={{0,30},{2,0},{4,2},{6,4},{8,6},{10,8},{12,10},{14,12},{16,14},{18,... | collective-permute-start | bytes 98312 | tf_op jit(solution)/shard_map/ppermute | solution.py:20
  130.5 1.9 collective-permute-done.16
  132.4 5.7 %collective-permute-start.19 = (bf16[1,128,128]{2,1,0:T(8,128)(2,1)S(1)}, bf16[1,128,128]{2,1,0:T(8,128)(2,1)S(1)}, u32[]{:S(2)}, u32[]{:S(2)}) collective-permute-start(bf16[1,128,128]{2,1,0:T(8,128)(2,1)S(1)} %collective-permute-done.17), channel_id=1, source_target_pairs={{0,30},{2,0},{4,2},{6,4},{8,6},{10,8},{12,10},{14,12},{16,14},{18,... | collective-permute-start | bytes 98312 | tf_op jit(solution)/shard_map/ppermute | solution.py:20
  138.1 1.8 collective-permute-done.18
  139.9 5.7 %collective-permute-start.21 = (bf16[1,128,128]{2,1,0:T(8,128)(2,1)S(1)}, bf16[1,128,128]{2,1,0:T(8,128)(2,1)S(1)}, u32[]{:S(2)}, u32[]{:S(2)}) collective-permute-start(bf16[1,128,128]{2,1,0:T(8,128)(2,1)S(1)} %collective-permute-done.19), channel_id=1, source_target_pairs={{0,30},{2,0},{4,2},{6,4},{8,6},{10,8},{12,10},{14,12},{16,14},{18,... | collective-permute-start | bytes 98312 | tf_op jit(solution)/shard_map/ppermute | solution.py:20
  145.6 1.8 collective-permute-done.20
  147.5 5.7 %collective-permute-start.23 = (bf16[1,128,128]{2,1,0:T(8,128)(2,1)S(1)}, bf16[1,128,128]{2,1,0:T(8,128)(2,1)S(1)}, u32[]{:S(2)}, u32[]{:S(2)}) collective-permute-start(bf16[1,128,128]{2,1,0:T(8,128)(2,1)S(1)} %collective-permute-done.21), channel_id=1, source_target_pairs={{0,30},{2,0},{4,2},{6,4},{8,6},{10,8},{12,10},{14,12},{16,14},{18,... | collective-permute-start | bytes 98312 | tf_op jit(solution)/shard_map/ppermute | solution.py:20
  153.2 1.8 collective-permute-done.22
  155.0 5.7 %collective-permute-start.25 = (bf16[1,128,128]{2,1,0:T(8,128)(2,1)S(1)}, bf16[1,128,128]{2,1,0:T(8,128)(2,1)S(1)}, u32[]{:S(2)}, u32[]{:S(2)}) collective-permute-start(bf16[1,128,128]{2,1,0:T(8,128)(2,1)S(1)} %collective-permute-done.23), channel_id=1, source_target_pairs={{0,30},{2,0},{4,2},{6,4},{8,6},{10,8},{12,10},{14,12},{16,14},{18,... | collective-permute-start | bytes 98312 | tf_op jit(solution)/shard_map/ppermute | solution.py:20
  160.7 1.8 collective-permute-done.24
  162.5 5.7 %collective-permute-start.27 = (bf16[1,128,128]{2,1,0:T(8,128)(2,1)S(1)}, bf16[1,128,128]{2,1,0:T(8,128)(2,1)S(1)}, u32[]{:S(2)}, u32[]{:S(2)}) collective-permute-start(bf16[1,128,128]{2,1,0:T(8,128)(2,1)S(1)} %collective-permute-done.25), channel_id=1, source_target_pairs={{0,30},{2,0},{4,2},{6,4},{8,6},{10,8},{12,10},{14,12},{16,14},{18,... | collective-permute-start | bytes 98312 | tf_op jit(solution)/shard_map/ppermute | solution.py:20
  168.2 1.8 collective-permute-done.26
  170.0 7.5 %collective-permute-done.28 = bf16[1,128,128]{2,1,0:T(8,128)(2,1)S(1)} collective-permute-done((bf16[1,128,128]{2,1,0:T(8,128)(2,1)S(1)}, bf16[1,128,128]{2,1,0:T(8,128)(2,1)S(1)}, u32[]{:S(2)}, u32[]{:S(2)}) %collective-permute-start.28) | collective-permute-done | bytes 32800 | tf_op jit(solution)/shard_map/ppermute | solution.py:18
  177.6 7.5 %collective-permute-done.29 = bf16[1,128,128]{2,1,0:T(8,128)(2,1)S(1)} collective-permute-done((bf16[1,128,128]{2,1,0:T(8,128)(2,1)S(1)}, bf16[1,128,128]{2,1,0:T(8,128)(2,1)S(1)}, u32[]{:S(2)}, u32[]{:S(2)}) %collective-permute-start.29) | collective-permute-done | bytes 32800 | tf_op jit(solution)/shard_map/ppermute | solution.py:18
  185.0 0.7 add_convert_fusion
  185.7 0.1 pad_maximum_fusion.1
  185.8 0.7 fusion
  186.5 0.1 slice.33
  186.7 0.1 fusion.11
  186.8 0.2 pad_maximum_fusion
  186.9 2.6 %copy.10 = bf16[1024,1024]{1,0:T(8,128)(2,1)} copy(bf16[1024,1024]{0,1:T(8,128)(2,1)S(1)} %pad_maximum_fusion) | data formatting | bytes 4194304 | tf_op jit(solution)/shard_map/concatenate | solution.py:113
  (67 shorter events, 0.4 us)
Async XLA Ops:
  6.5 24.1 %all-reduce.3.cloned.1.call-start = ((), (), s32[]{:S(2)}) async-start(), calls=%async_computation | async-start | bytes 524288 | tf_op jit(solution)/shard_map/psum | solution.py:28
  9.3 105.8 %all-reduce.5.cloned.1.call-start = ((), (), s32[]{:S(2)}) async-start(), calls=%async_computation.1 | async-start | bytes 524288 | tf_op jit(solution)/shard_map/psum | solution.py:28
  10.6 88.1 %copy-start.2 = (bf16[2,128,128]{2,1,0:T(8,128)(2,1)S(1)}, bf16[2,128,128]{2,1,0:T(8,128)(2,1)}, u32[]{:S(2)}) copy-start(bf16[2,128,128]{2,1,0:T(8,128)(2,1)} %param.7) | copy-start | bytes 196612
  30.7 68.0 %copy-start = (bf16[1024,128]{0,1:T(8,128)(2,1)S(1)}, bf16[1024,128]{0,1:T(8,128)(2,1)}, u32[]{:S(2)}) copy-start(bf16[1024,128]{0,1:T(8,128)(2,1)} %all-reduce.3.cloned.1.call-done) | copy-start | bytes 786436
  32.1 7.1 %collective-permute-start = (bf16[1,128,128]{2,1,0:T(8,128)(2,1)S(1)}, bf16[1,128,128]{2,1,0:T(8,128)(2,1)S(1)}, u32[]{:S(2)}, u32[]{:S(2)}) collective-permute-start(bf16[1,128,128]{2,1,0:T(8,128)(2,1)S(1)} %get-tuple-element.8), channel_id=1, source_target_pairs={{0,30},{2,0},{4,2},{6,4},{8,6},{10,8},{12,10},{14,12},{16,14},{18,... | collective-permute-start | bytes 98312 | tf_op jit(solution)/shard_map/ppermute | solution.py:20
  37.6 7.6 %collective-permute-start.1 = (bf16[1,128,128]{2,1,0:T(8,128)(2,1)S(1)}, bf16[1,128,128]{2,1,0:T(8,128)(2,1)S(1)}, u32[]{:S(2)}, u32[]{:S(2)}) collective-permute-start(bf16[1,128,128]{2,1,0:T(8,128)(2,1)S(1)} %get-tuple-element.8), channel_id=1, source_target_pairs={{0,2},{2,4},{4,6},{6,8},{8,10},{10,12},{12,14},{14,16},{16,18},{18... | collective-permute-start | bytes 98312 | tf_op jit(solution)/shard_map/ppermute | solution.py:18
  39.2 7.5 %collective-permute-start.2 = (bf16[1,128,128]{2,1,0:T(8,128)(2,1)S(1)}, bf16[1,128,128]{2,1,0:T(8,128)(2,1)S(1)}, u32[]{:S(2)}, u32[]{:S(2)}) collective-permute-start(bf16[1,128,128]{2,1,0:T(8,128)(2,1)S(1)} %collective-permute-done), channel_id=1, source_target_pairs={{0,30},{2,0},{4,2},{6,4},{8,6},{10,8},{12,10},{14,12},{16,14},{18,... | collective-permute-start | bytes 98312 | tf_op jit(solution)/shard_map/ppermute | solution.py:20
  45.2 7.5 %collective-permute-start.3 = (bf16[1,128,128]{2,1,0:T(8,128)(2,1)S(1)}, bf16[1,128,128]{2,1,0:T(8,128)(2,1)S(1)}, u32[]{:S(2)}, u32[]{:S(2)}) collective-permute-start(bf16[1,128,128]{2,1,0:T(8,128)(2,1)S(1)} %collective-permute-done.1), channel_id=1, source_target_pairs={{0,2},{2,4},{4,6},{6,8},{8,10},{10,12},{12,14},{14,16},{16,18},{18... | collective-permute-start | bytes 98312 | tf_op jit(solution)/shard_map/ppermute | solution.py:18
  46.7 7.5 %collective-permute-start.4 = (bf16[1,128,128]{2,1,0:T(8,128)(2,1)S(1)}, bf16[1,128,128]{2,1,0:T(8,128)(2,1)S(1)}, u32[]{:S(2)}, u32[]{:S(2)}) collective-permute-start(bf16[1,128,128]{2,1,0:T(8,128)(2,1)S(1)} %collective-permute-done.2), channel_id=1, source_target_pairs={{0,30},{2,0},{4,2},{6,4},{8,6},{10,8},{12,10},{14,12},{16,14},{18,... | collective-permute-start | bytes 98312 | tf_op jit(solution)/shard_map/ppermute | solution.py:20
  52.7 7.5 %collective-permute-start.5 = (bf16[1,128,128]{2,1,0:T(8,128)(2,1)S(1)}, bf16[1,128,128]{2,1,0:T(8,128)(2,1)S(1)}, u32[]{:S(2)}, u32[]{:S(2)}) collective-permute-start(bf16[1,128,128]{2,1,0:T(8,128)(2,1)S(1)} %collective-permute-done.3), channel_id=1, source_target_pairs={{0,2},{2,4},{4,6},{6,8},{8,10},{10,12},{12,14},{14,16},{16,18},{18... | collective-permute-start | bytes 98312 | tf_op jit(solution)/shard_map/ppermute | solution.py:18
  54.2 7.5 %collective-permute-start.6 = (bf16[1,128,128]{2,1,0:T(8,128)(2,1)S(1)}, bf16[1,128,128]{2,1,0:T(8,128)(2,1)S(1)}, u32[]{:S(2)}, u32[]{:S(2)}) collective-permute-start(bf16[1,128,128]{2,1,0:T(8,128)(2,1)S(1)} %collective-permute-done.4), channel_id=1, source_target_pairs={{0,30},{2,0},{4,2},{6,4},{8,6},{10,8},{12,10},{14,12},{16,14},{18,... | collective-permute-start | bytes 98312 | tf_op jit(solution)/shard_map/ppermute | solution.py:20
  60.2 7.5 %collective-permute-start.7 = (bf16[1,128,128]{2,1,0:T(8,128)(2,1)S(1)}, bf16[1,128,128]{2,1,0:T(8,128)(2,1)S(1)}, u32[]{:S(2)}, u32[]{:S(2)}) collective-permute-start(bf16[1,128,128]{2,1,0:T(8,128)(2,1)S(1)} %collective-permute-done.5), channel_id=1, source_target_pairs={{0,2},{2,4},{4,6},{6,8},{8,10},{10,12},{12,14},{14,16},{16,18},{18... | collective-permute-start | bytes 98312 | tf_op jit(solution)/shard_map/ppermute | solution.py:18
  61.7 7.5 %collective-permute-start.8 = (bf16[1,128,128]{2,1,0:T(8,128)(2,1)S(1)}, bf16[1,128,128]{2,1,0:T(8,128)(2,1)S(1)}, u32[]{:S(2)}, u32[]{:S(2)}) collective-permute-start(bf16[1,128,128]{2,1,0:T(8,128)(2,1)S(1)} %collective-permute-done.6), channel_id=1, source_target_pairs={{0,30},{2,0},{4,2},{6,4},{8,6},{10,8},{12,10},{14,12},{16,14},{18,... | collective-permute-start | bytes 98312 | tf_op jit(solution)/shard_map/ppermute | solution.py:20
  67.7 7.5 %collective-permute-start.9 = (bf16[1,128,128]{2,1,0:T(8,128)(2,1)S(1)}, bf16[1,128,128]{2,1,0:T(8,128)(2,1)S(1)}, u32[]{:S(2)}, u32[]{:S(2)}) collective-permute-start(bf16[1,128,128]{2,1,0:T(8,128)(2,1)S(1)} %collective-permute-done.7), channel_id=1, source_target_pairs={{0,2},{2,4},{4,6},{6,8},{8,10},{10,12},{12,14},{14,16},{16,18},{18... | collective-permute-start | bytes 98312 | tf_op jit(solution)/shard_map/ppermute | solution.py:18
  69.2 7.6 %collective-permute-start.10 = (bf16[1,128,128]{2,1,0:T(8,128)(2,1)S(1)}, bf16[1,128,128]{2,1,0:T(8,128)(2,1)S(1)}, u32[]{:S(2)}, u32[]{:S(2)}) collective-permute-start(bf16[1,128,128]{2,1,0:T(8,128)(2,1)S(1)} %collective-permute-done.8), channel_id=1, source_target_pairs={{0,30},{2,0},{4,2},{6,4},{8,6},{10,8},{12,10},{14,12},{16,14},{18,... | collective-permute-start | bytes 98312 | tf_op jit(solution)/shard_map/ppermute | solution.py:20
  75.2 7.7 %collective-permute-start.11 = (bf16[1,128,128]{2,1,0:T(8,128)(2,1)S(1)}, bf16[1,128,128]{2,1,0:T(8,128)(2,1)S(1)}, u32[]{:S(2)}, u32[]{:S(2)}) collective-permute-start(bf16[1,128,128]{2,1,0:T(8,128)(2,1)S(1)} %collective-permute-done.9), channel_id=1, source_target_pairs={{0,2},{2,4},{4,6},{6,8},{8,10},{10,12},{12,14},{14,16},{16,18},{18... | collective-permute-start | bytes 98312 | tf_op jit(solution)/shard_map/ppermute | solution.py:18
  76.9 13.7 %collective-permute-start.12 = (bf16[1,128,128]{2,1,0:T(8,128)(2,1)S(1)}, bf16[1,128,128]{2,1,0:T(8,128)(2,1)S(1)}, u32[]{:S(2)}, u32[]{:S(2)}) collective-permute-start(bf16[1,128,128]{2,1,0:T(8,128)(2,1)S(1)} %collective-permute-done.10), channel_id=1, source_target_pairs={{0,30},{2,0},{4,2},{6,4},{8,6},{10,8},{12,10},{14,12},{16,14},{18,... | collective-permute-start | bytes 98312 | tf_op jit(solution)/shard_map/ppermute | solution.py:20
  82.9 7.6 %collective-permute-start.13 = (bf16[1,128,128]{2,1,0:T(8,128)(2,1)S(1)}, bf16[1,128,128]{2,1,0:T(8,128)(2,1)S(1)}, u32[]{:S(2)}, u32[]{:S(2)}) collective-permute-start(bf16[1,128,128]{2,1,0:T(8,128)(2,1)S(1)} %collective-permute-done.11), channel_id=1, source_target_pairs={{0,2},{2,4},{4,6},{6,8},{8,10},{10,12},{12,14},{14,16},{16,18},{18... | collective-permute-start | bytes 98312 | tf_op jit(solution)/shard_map/ppermute | solution.py:18
  90.5 7.5 %collective-permute-start.14 = (bf16[1,128,128]{2,1,0:T(8,128)(2,1)S(1)}, bf16[1,128,128]{2,1,0:T(8,128)(2,1)S(1)}, u32[]{:S(2)}, u32[]{:S(2)}) collective-permute-start(bf16[1,128,128]{2,1,0:T(8,128)(2,1)S(1)} %collective-permute-done.13), channel_id=1, source_target_pairs={{0,2},{2,4},{4,6},{6,8},{8,10},{10,12},{12,14},{14,16},{16,18},{18... | collective-permute-start | bytes 98312 | tf_op jit(solution)/shard_map/ppermute | solution.py:18
  116.5 8.4 %collective-permute-start.15 = (bf16[1,128,128]{2,1,0:T(8,128)(2,1)S(1)}, bf16[1,128,128]{2,1,0:T(8,128)(2,1)S(1)}, u32[]{:S(2)}, u32[]{:S(2)}) collective-permute-start(bf16[1,128,128]{2,1,0:T(8,128)(2,1)S(1)} %get-tuple-element.6), channel_id=1, source_target_pairs={{0,30},{2,0},{4,2},{6,4},{8,6},{10,8},{12,10},{14,12},{16,14},{18,... | collective-permute-start | bytes 98312 | tf_op jit(solution)/shard_map/ppermute | solution.py:20
  124.8 61.0 %copy-start.1 = (bf16[1024,128]{0,1:T(8,128)(2,1)S(1)}, bf16[1024,128]{0,1:T(8,128)(2,1)}, u32[]{:S(2)}) copy-start(bf16[1024,128]{0,1:T(8,128)(2,1)} %all-reduce.5.cloned.1.call-done) | copy-start | bytes 786436
  124.8 7.6 %collective-permute-start.16 = (bf16[1,128,128]{2,1,0:T(8,128)(2,1)S(1)}, bf16[1,128,128]{2,1,0:T(8,128)(2,1)S(1)}, u32[]{:S(2)}, u32[]{:S(2)}) collective-permute-start(bf16[1,128,128]{2,1,0:T(8,128)(2,1)S(1)} %get-tuple-element.6), channel_id=1, source_target_pairs={{0,2},{2,4},{4,6},{6,8},{8,10},{10,12},{12,14},{14,16},{16,18},{18... | collective-permute-start | bytes 98312 | tf_op jit(solution)/shard_map/ppermute | solution.py:18
  124.9 7.5 %collective-permute-start.17 = (bf16[1,128,128]{2,1,0:T(8,128)(2,1)S(1)}, bf16[1,128,128]{2,1,0:T(8,128)(2,1)S(1)}, u32[]{:S(2)}, u32[]{:S(2)}) collective-permute-start(bf16[1,128,128]{2,1,0:T(8,128)(2,1)S(1)} %collective-permute-done.15), channel_id=1, source_target_pairs={{0,30},{2,0},{4,2},{6,4},{8,6},{10,8},{12,10},{14,12},{16,14},{18,... | collective-permute-start | bytes 98312 | tf_op jit(solution)/shard_map/ppermute | solution.py:20
  132.4 7.5 %collective-permute-start.18 = (bf16[1,128,128]{2,1,0:T(8,128)(2,1)S(1)}, bf16[1,128,128]{2,1,0:T(8,128)(2,1)S(1)}, u32[]{:S(2)}, u32[]{:S(2)}) collective-permute-start(bf16[1,128,128]{2,1,0:T(8,128)(2,1)S(1)} %collective-permute-done.16), channel_id=1, source_target_pairs={{0,2},{2,4},{4,6},{6,8},{8,10},{10,12},{12,14},{14,16},{16,18},{18... | collective-permute-start | bytes 98312 | tf_op jit(solution)/shard_map/ppermute | solution.py:18
  132.4 7.5 %collective-permute-start.19 = (bf16[1,128,128]{2,1,0:T(8,128)(2,1)S(1)}, bf16[1,128,128]{2,1,0:T(8,128)(2,1)S(1)}, u32[]{:S(2)}, u32[]{:S(2)}) collective-permute-start(bf16[1,128,128]{2,1,0:T(8,128)(2,1)S(1)} %collective-permute-done.17), channel_id=1, source_target_pairs={{0,30},{2,0},{4,2},{6,4},{8,6},{10,8},{12,10},{14,12},{16,14},{18,... | collective-permute-start | bytes 98312 | tf_op jit(solution)/shard_map/ppermute | solution.py:20
  139.9 7.5 %collective-permute-start.20 = (bf16[1,128,128]{2,1,0:T(8,128)(2,1)S(1)}, bf16[1,128,128]{2,1,0:T(8,128)(2,1)S(1)}, u32[]{:S(2)}, u32[]{:S(2)}) collective-permute-start(bf16[1,128,128]{2,1,0:T(8,128)(2,1)S(1)} %collective-permute-done.18), channel_id=1, source_target_pairs={{0,2},{2,4},{4,6},{6,8},{8,10},{10,12},{12,14},{14,16},{16,18},{18... | collective-permute-start | bytes 98312 | tf_op jit(solution)/shard_map/ppermute | solution.py:18
  139.9 7.5 %collective-permute-start.21 = (bf16[1,128,128]{2,1,0:T(8,128)(2,1)S(1)}, bf16[1,128,128]{2,1,0:T(8,128)(2,1)S(1)}, u32[]{:S(2)}, u32[]{:S(2)}) collective-permute-start(bf16[1,128,128]{2,1,0:T(8,128)(2,1)S(1)} %collective-permute-done.19), channel_id=1, source_target_pairs={{0,30},{2,0},{4,2},{6,4},{8,6},{10,8},{12,10},{14,12},{16,14},{18,... | collective-permute-start | bytes 98312 | tf_op jit(solution)/shard_map/ppermute | solution.py:20
  147.4 7.5 %collective-permute-start.22 = (bf16[1,128,128]{2,1,0:T(8,128)(2,1)S(1)}, bf16[1,128,128]{2,1,0:T(8,128)(2,1)S(1)}, u32[]{:S(2)}, u32[]{:S(2)}) collective-permute-start(bf16[1,128,128]{2,1,0:T(8,128)(2,1)S(1)} %collective-permute-done.20), channel_id=1, source_target_pairs={{0,2},{2,4},{4,6},{6,8},{8,10},{10,12},{12,14},{14,16},{16,18},{18... | collective-permute-start | bytes 98312 | tf_op jit(solution)/shard_map/ppermute | solution.py:18
  147.5 7.5 %collective-permute-start.23 = (bf16[1,128,128]{2,1,0:T(8,128)(2,1)S(1)}, bf16[1,128,128]{2,1,0:T(8,128)(2,1)S(1)}, u32[]{:S(2)}, u32[]{:S(2)}) collective-permute-start(bf16[1,128,128]{2,1,0:T(8,128)(2,1)S(1)} %collective-permute-done.21), channel_id=1, source_target_pairs={{0,30},{2,0},{4,2},{6,4},{8,6},{10,8},{12,10},{14,12},{16,14},{18,... | collective-permute-start | bytes 98312 | tf_op jit(solution)/shard_map/ppermute | solution.py:20
  154.9 7.5 %collective-permute-start.24 = (bf16[1,128,128]{2,1,0:T(8,128)(2,1)S(1)}, bf16[1,128,128]{2,1,0:T(8,128)(2,1)S(1)}, u32[]{:S(2)}, u32[]{:S(2)}) collective-permute-start(bf16[1,128,128]{2,1,0:T(8,128)(2,1)S(1)} %collective-permute-done.22), channel_id=1, source_target_pairs={{0,2},{2,4},{4,6},{6,8},{8,10},{10,12},{12,14},{14,16},{16,18},{18... | collective-permute-start | bytes 98312 | tf_op jit(solution)/shard_map/ppermute | solution.py:18
  155.0 7.5 %collective-permute-start.25 = (bf16[1,128,128]{2,1,0:T(8,128)(2,1)S(1)}, bf16[1,128,128]{2,1,0:T(8,128)(2,1)S(1)}, u32[]{:S(2)}, u32[]{:S(2)}) collective-permute-start(bf16[1,128,128]{2,1,0:T(8,128)(2,1)S(1)} %collective-permute-done.23), channel_id=1, source_target_pairs={{0,30},{2,0},{4,2},{6,4},{8,6},{10,8},{12,10},{14,12},{16,14},{18,... | collective-permute-start | bytes 98312 | tf_op jit(solution)/shard_map/ppermute | solution.py:20
  162.5 7.5 %collective-permute-start.26 = (bf16[1,128,128]{2,1,0:T(8,128)(2,1)S(1)}, bf16[1,128,128]{2,1,0:T(8,128)(2,1)S(1)}, u32[]{:S(2)}, u32[]{:S(2)}) collective-permute-start(bf16[1,128,128]{2,1,0:T(8,128)(2,1)S(1)} %collective-permute-done.24), channel_id=1, source_target_pairs={{0,2},{2,4},{4,6},{6,8},{8,10},{10,12},{12,14},{14,16},{16,18},{18... | collective-permute-start | bytes 98312 | tf_op jit(solution)/shard_map/ppermute | solution.py:18
  162.5 15.1 %collective-permute-start.27 = (bf16[1,128,128]{2,1,0:T(8,128)(2,1)S(1)}, bf16[1,128,128]{2,1,0:T(8,128)(2,1)S(1)}, u32[]{:S(2)}, u32[]{:S(2)}) collective-permute-start(bf16[1,128,128]{2,1,0:T(8,128)(2,1)S(1)} %collective-permute-done.25), channel_id=1, source_target_pairs={{0,30},{2,0},{4,2},{6,4},{8,6},{10,8},{12,10},{14,12},{16,14},{18,... | collective-permute-start | bytes 98312 | tf_op jit(solution)/shard_map/ppermute | solution.py:20
  170.0 7.5 %collective-permute-start.28 = (bf16[1,128,128]{2,1,0:T(8,128)(2,1)S(1)}, bf16[1,128,128]{2,1,0:T(8,128)(2,1)S(1)}, u32[]{:S(2)}, u32[]{:S(2)}) collective-permute-start(bf16[1,128,128]{2,1,0:T(8,128)(2,1)S(1)} %collective-permute-done.26), channel_id=1, source_target_pairs={{0,2},{2,4},{4,6},{6,8},{8,10},{10,12},{12,14},{14,16},{16,18},{18... | collective-permute-start | bytes 98312 | tf_op jit(solution)/shard_map/ppermute | solution.py:18
  177.5 7.5 %collective-permute-start.29 = (bf16[1,128,128]{2,1,0:T(8,128)(2,1)S(1)}, bf16[1,128,128]{2,1,0:T(8,128)(2,1)S(1)}, u32[]{:S(2)}, u32[]{:S(2)}) collective-permute-start(bf16[1,128,128]{2,1,0:T(8,128)(2,1)S(1)} %collective-permute-done.28), channel_id=1, source_target_pairs={{0,2},{2,4},{4,6},{6,8},{8,10},{10,12},{12,14},{14,16},{16,18},{18... | collective-permute-start | bytes 98312 | tf_op jit(solution)/shard_map/ppermute | solution.py:18
Sparse Core Ops, SparseCore 0:
  9.7 20.9 all-reduce.2
  101.0 14.1 all-reduce.4
